TPU v7x, 512 devices: a whole 4x4x16 slice. The times are simulated.
512 devices in a mesh: pipe: 4 (over y), expert: 32 (over z, core), tensor: 4 (over x).
Axes of the slice: x: 4, y: 4, z: 16, core: 2. Of those that a mesh axis runs over, the one named last changes fastest.
Arguments:
- tokens: bfloat16 [512, 6144], P('expert', ('pipe', 'tensor')), may hold values from -6 to 6
- expert_ids: int32 [512, 2], P('expert'), may hold values from 0 to 7, all different within a row; in each aligned block of 16 rows (0 to 15, 16 to 31, ...) at most 5 rows name the same one
- gates: float32 [512, 2], P('expert'), may hold values from 0.2 to 1
- w_gate: bfloat16 [32, 6144, 2048], P('expert', None, ('pipe', 'tensor')), may hold values from -0.078125 to 0.078125
- w_up: bfloat16 [32, 6144, 2048], P('expert', None, ('pipe', 'tensor')), may hold values from -0.078125 to 0.078125
- w_down: bfloat16 [32, 2048, 6144], P('expert', ('pipe', 'tensor')), may hold values from -0.0625 to 0.0625
- d_out: bfloat16 [512, 6144], P('expert', ('pipe', 'tensor')), may hold values from -6 to 6
Outputs:
- moe_out: bfloat16 [512, 6144], P('expert', ('pipe', 'tensor'))
- grad_tokens: bfloat16 [512, 6144], P('expert', ('pipe', 'tensor'))
- grad_gates: float32 [512, 2], P('expert')
Inputs may be any that keep to these rules, and one draw needn't show every extreme that they name: `expert_ids`: each row names 2 different experts. Among the rows of one index of expert (aligned blocks of 16 rows) no expert is named more than 5 times, a bound that some block reaches.
All inputs are finite; a program needn't handle non-finite values.
Results may differ from a plain program's by a relative error of at most 0.017.
Values may be sent and summed in bfloat16 or wider, within the bound.
No kernel may reach another device: no remote copies, remote signals or barrier semaphores. Data moves between devices by JAX's collectives and lax.ppermute only.
A program may use at most 64 MiB of HBM per device.

v0:
```python
import jax
import jax.numpy as jnp
from jax import lax
from jax.sharding import PartitionSpec as P


def per_device(tokens, expert_ids, gates, w_gate, w_up, w_down, d_out):
    tok_rows = tokens.shape[0]
    feat = tokens.shape[1]
    top = expert_ids.shape[1]
    devices_all = lax.axis_size("expert")
    experts = min(8, devices_all)
    group = devices_all // experts
    capacity = min(
        tok_rows,
        max(2, max(5 * tok_rows * top // (4 * experts), (tok_rows * top + experts - 1) // experts)),
    )
    slots = experts * capacity
    flat_ids = expert_ids.reshape(-1)
    onehot = (flat_ids[:, None] == jnp.arange(experts, dtype=jnp.int32)[None, :]).astype(jnp.int32)
    position = jnp.sum(jnp.cumsum(onehot, axis=0) * onehot, axis=1) - 1
    slot_of = flat_ids * capacity + position
    picks = (jnp.arange(slots, dtype=jnp.int32)[:, None] == slot_of[None, :]).astype(jnp.float32)
    pick_rows = picks.reshape(slots, tok_rows, top)
    select_tok = jnp.sum(pick_rows, axis=2).astype(jnp.bfloat16)
    select_gate = jnp.sum(pick_rows * gates[None, :, :], axis=2)
    picked = jnp.dot(select_tok, tokens, preferred_element_type=jnp.float32).astype(jnp.bfloat16)
    scaled = jnp.dot(
        select_gate, d_out.astype(jnp.float32), precision=lax.Precision.HIGHEST
    ).astype(jnp.bfloat16)
    send = jnp.concatenate([picked, scaled], axis=1).reshape(experts, capacity, 2 * feat)
    send = jnp.repeat(send, group, axis=0)
    recv = lax.all_to_all(send, "expert", split_axis=0, concat_axis=0, tiled=True)
    recv = recv.reshape(devices_all * capacity, 2 * feat)
    part_x = recv[:, :feat]
    part_dy = recv[:, feat:]
    rows_x = lax.all_gather(part_x, ("pipe", "tensor"), axis=1, tiled=True)
    rows_dy = lax.all_gather(part_dy, ("pipe", "tensor"), axis=1, tiled=True)
    gate_proj = w_gate[0]
    up_proj = w_up[0]
    down_proj = w_down[0]
    contract_last = (((1,), (1,)), ((), ()))
    h_gate = jnp.dot(rows_x, gate_proj, preferred_element_type=jnp.float32)
    h_up = jnp.dot(rows_x, up_proj, preferred_element_type=jnp.float32)
    sig = jax.nn.sigmoid(h_gate)
    hidden = (h_gate * sig * h_up).astype(jnp.bfloat16)
    out_terms = jnp.dot(hidden, down_proj, preferred_element_type=jnp.float32)
    d_hidden = lax.dot_general(
        rows_dy, down_proj, contract_last, preferred_element_type=jnp.float32
    )
    d_gate_h = (d_hidden * h_up * sig * (1.0 + h_gate * (1.0 - sig))).astype(jnp.bfloat16)
    d_up_h = (d_hidden * h_gate * sig).astype(jnp.bfloat16)
    dx_terms = lax.dot_general(
        d_gate_h, gate_proj, contract_last, preferred_element_type=jnp.float32
    )
    dx_terms = dx_terms + lax.dot_general(
        d_up_h, up_proj, contract_last, preferred_element_type=jnp.float32
    )
    out_share = lax.psum_scatter(
        out_terms.astype(jnp.bfloat16), ("pipe", "tensor"), scatter_dimension=1, tiled=True
    )
    dx_share = lax.psum_scatter(
        dx_terms.astype(jnp.bfloat16), ("pipe", "tensor"), scatter_dimension=1, tiled=True
    )
    back_send = jnp.concatenate([out_share, dx_share], axis=1).reshape(
        devices_all, capacity, 2 * feat
    )
    back = lax.all_to_all(back_send, "expert", split_axis=0, concat_axis=0, tiled=True)
    back_rows = (
        jnp.sum(back.astype(jnp.float32).reshape(experts, group, capacity, 2 * feat), axis=1)
        .astype(jnp.bfloat16)
        .reshape(slots, 2 * feat)
    )
    assign = picks.T.astype(jnp.bfloat16)
    a_both = jnp.dot(assign, back_rows, preferred_element_type=jnp.float32)
    a_out = a_both[:, :feat].reshape(tok_rows, top, feat)
    a_dx = a_both[:, feat:].reshape(tok_rows, top, feat)
    moe_out = jnp.sum(gates[:, :, None] * a_out, axis=1).astype(jnp.bfloat16)
    grad_tokens = jnp.sum(a_dx, axis=1).astype(jnp.bfloat16)
    partial_dots = jnp.sum(d_out.astype(jnp.float32)[:, None, :] * a_out, axis=2)
    grad_gates = lax.psum(partial_dots, ("pipe", "tensor"))
    return (moe_out, grad_tokens, grad_gates)


def solution(mesh):
    return jax.shard_map(
        per_device,
        mesh=mesh,
        in_specs=(
            P("expert", ("pipe", "tensor")),
            P("expert", None),
            P("expert", None),
            P("expert", None, ("pipe", "tensor")),
            P("expert", None, ("pipe", "tensor")),
            P("expert", ("pipe", "tensor"), None),
            P("expert", ("pipe", "tensor")),
        ),
        out_specs=(
            P("expert", ("pipe", "tensor")),
            P("expert", ("pipe", "tensor")),
            P("expert", None),
        ),
        check_vma=False,
    )
```

profile of v0, /device:TPU:32, one launch (start us, length us, event | category | flops | bytes accessed | tf_op | source)
XLA Modules:
  0.0 457.4 jit_solution(14242704866884179317)
XLA Ops:
  7.2 0.9 copy.35
  8.3 0.2 select_reduce_fusion.1
  8.7 0.7 multiply_add_fusion
  9.4 0.8 convert_reduce_fusion
  10.1 0.9 convolution_convert_fusion.1
  11.1 0.9 convolution_convert_fusion.2
  12.1 41.8 %all_to_all.10 = bf16[32,5,768]{2,1,0:T(8,128)(2,1)S(1)} all-to-all(bf16[32,5,768]{2,1,0:T(8,128)(2,1)S(1)} %bitcast.32), channel_id=1, replica_groups=mesh['pipe'=4,'expert'=32,'tensor'=4] {'expert'}, dimensions={0} | all-to-all | bytes 491520 | tf_op jit(solution)/shard_map/all_to_all | solution.py:33
  54.0 0.7 fusion.21
  54.8 0.7 all-gather.5.cloned.1.call-update
  55.6 54.5 %all-gather.3.cloned.1.call-done = bf16[160,6144]{1,0:T(8,128)(2,1)} async-done(((bf16[160,384]{1,0:T(8,128)(2,1)}), bf16[160,6144]{1,0:T(8,128)(2,1)}) %all-gather.3.cloned.1.call-update) | async-done | bytes 1966096 | tf_op jit(solution)/shard_map/all_gather | solution.py:37
  110.0 2.3 fusion.9
  112.4 2.2 fusion.5
  114.6 60.3 %all-gather.5.cloned.1.call-done = bf16[160,6144]{1,0:T(8,128)(2,1)} async-done(((bf16[160,384]{1,0:T(8,128)(2,1)}), bf16[160,6144]{1,0:T(8,128)(2,1)}) %all-gather.5.cloned.1.call-update) | async-done | bytes 1966096 | tf_op jit(solution)/shard_map/all_gather | solution.py:38
  174.9 2.2 fusion.1
  177.1 0.7 fusion.7
  177.8 0.7 copy-done.3
  178.5 1.6 fusion
  180.1 2.8 copy.40
  182.9 2.2 convolution_convert_fusion
  185.1 2.8 copy.38
  187.9 85.6 %reduce-scatter.9.cloned.1.call-done = bf16[384,160]{1,0:T(8,128)(2,1)} async-done(((bf16[6144,160]{1,0:T(8,128)(2,1)}), bf16[384,160]{1,0:T(8,128)(2,1)}) %reduce-scatter.9.cloned.1.call-update) | async-done | bytes 122896
  273.6 1.1 copy.41
  274.6 93.5 %reduce-scatter.7.cloned.1.call-done = bf16[384,160]{1,0:T(8,128)(2,1)} async-done(((bf16[6144,160]{1,0:T(8,128)(2,1)}), bf16[384,160]{1,0:T(8,128)(2,1)}) %reduce-scatter.7.cloned.1.call-update) | async-done | bytes 122896
  368.1 1.1 copy.39
  369.2 0.8 reshape.67
  370.1 12.8 %all-to-all-start.1 = ((bf16[32,5,768]{2,1,0:T(8,128)(2,1)}), bf16[32,5,768]{2,1,0:T(8,128)(2,1)S(1)}, u32[]{:S(2)}, u32[]{:S(2)}) async-start(bf16[32,5,768]{2,1,0:T(8,128)(2,1)} %reshape.67), calls=%async_computation.1 | async-start | bytes 786432 | tf_op jit(solution)/shard_map/all_to_all | solution.py:68
  383.0 26.5 %all-to-all-done.1 = bf16[32,5,768]{2,1,0:T(8,128)(2,1)S(1)} async-done(((bf16[32,5,768]{2,1,0:T(8,128)(2,1)}), bf16[32,5,768]{2,1,0:T(8,128)(2,1)S(1)}, u32[]{:S(2)}, u32[]{:S(2)}) %all-to-all-start.1) | async-done | bytes 245792 | tf_op jit(solution)/shard_map/all_to_all | solution.py:68
  409.7 0.2 fusion.15
  410.2 38.6 %psum.7 = f32[16,2]{1,0:T(8,128)S(1)} all-reduce(f32[16,2]{1,0:T(8,128)S(1)} %reduce_sum.72), channel_id=1, replica_groups=mesh['pipe'=4,'expert'=32,'tensor'=4] {'pipe','tensor'}, use_global_device_ids=true, to_apply=%region_10.11 | all-reduce | flops 32 | bytes 256 | tf_op jit(solution)/shard_map/psum | solution.py:81
  448.8 0.6 copy.37
  449.5 0.7 multiply_reduce_fusion.1
  450.2 0.7 reduce_sum.70
  (42 shorter events, 1.4 us)
Async XLA Ops:
  7.2 102.9 %copy-start = (bf16[1,6144,128]{2,1,0:T(8,128)(2,1)S(1)}, bf16[1,6144,128]{2,1,0:T(8,128)(2,1)}, u32[]{:S(2)}) copy-start(bf16[1,6144,128]{2,1,0:T(8,128)(2,1)} %param.10) | copy-start | bytes 4718596
  7.2 102.8 %all-gather.3.cloned.1.call-start = ((), (), s32[]{:S(2)}) async-start(), calls=%async_computation.4 | async-start | bytes 2088960 | tf_op jit(solution)/shard_map/all_gather | solution.py:37
  54.8 120.1 %all-gather.5.cloned.1.call-start = ((), (), s32[]{:S(2)}) async-start(), calls=%async_computation.5 | async-start | bytes 2088960 | tf_op jit(solution)/shard_map/all_gather | solution.py:38
  55.5 218.1 %reduce-scatter.9.cloned.1.call-start = ((), (), s32[]{:S(2)}) async-start(), calls=%async_computation.7 | async-start | bytes 3342336
  110.0 2.4 copy-start.1
  112.4 64.7 %copy-start.4 = (f32[160,128]{1,0:T(8,128)}, f32[160,128]{1,0:T(8,128)S(1)}, u32[]{:S(2)}) copy-start(f32[160,128]{1,0:T(8,128)S(1)} %fusion.9) | copy-start | bytes 245764
  112.4 62.5 %copy-start.2 = (bf16[1,128,6144]{2,1,0:T(8,128)(2,1)S(1)}, bf16[1,128,6144]{2,1,0:T(8,128)(2,1)}, u32[]{:S(2)}) copy-start(bf16[1,128,6144]{2,1,0:T(8,128)(2,1)} %param.12) | copy-start | bytes 4718596
  114.6 62.5 %copy-start.5 = (f32[160,128]{1,0:T(8,128)}, f32[160,128]{1,0:T(8,128)S(1)}, u32[]{:S(2)}) copy-start(f32[160,128]{1,0:T(8,128)S(1)} %fusion.5) | copy-start | bytes 245764
  177.1 1.4 copy-start.3
  182.9 185.2 %reduce-scatter.7.cloned.1.call-start = ((), (), s32[]{:S(2)}) async-start(), calls=%async_computation.6 | async-start | bytes 3342336
  187.9 195.0 %copy-start.7 = (f32[16,2]{0,1:T(2,128)S(1)}, f32[16,2]{0,1:T(2,128)}, u32[]{:S(2)}) copy-start(f32[16,2]{0,1:T(2,128)} %param.9) | copy-start | bytes 388
  187.9 195.1 %copy-start.6 = (bf16[16,384]{1,0:T(8,128)(2,1)S(1)}, bf16[16,384]{1,0:T(8,128)(2,1)}, u32[]{:S(2)}) copy-start(bf16[16,384]{1,0:T(8,128)(2,1)} %param.13) | copy-start | bytes 36868
  370.1 39.5 %all-to-all-start.1 = ((bf16[32,5,768]{2,1,0:T(8,128)(2,1)}), bf16[32,5,768]{2,1,0:T(8,128)(2,1)S(1)}, u32[]{:S(2)}, u32[]{:S(2)}) async-start(bf16[32,5,768]{2,1,0:T(8,128)(2,1)} %reshape.67), calls=%async_computation.1 | async-start | bytes 786432 | tf_op jit(solution)/shard_map/all_to_all | solution.py:68
Sparse Core Ops, SparseCore 0:
  54.9 55.0 all-gather.2
  113.0 61.8 all-gather.4
  183.0 90.5 reduce-scatter.8
  277.6 90.4 reduce-scatter.6
where the time goes:
time: 458 us; the launch traced here: 457 us
  waiting for transfers between devices  321 us (70%)
  blocking collectives  80.5 us (18%)
  between operations  14 us (3%)
  matrix products  13.2 us (3%)
  starting transfers between devices  13 us (3%)
  local copies, waits for them, and re-layouts  12.2 us (3%)
    unnamed x6, waiting for transfers between devices  180 us
    all_gather x1, waiting for transfers between devices, per_device(): rows_dy = lax.all_gather(part_dy, ('pipe', 'tensor'), axis=1, tiled=True)  60.3 us
    all_gather x1, waiting for transfers between devices, per_device(): rows_x = lax.all_gather(part_x, ('pipe', 'tensor'), axis=1, tiled=True)  54.5 us
    all_to_all x1, blocking collectives, per_device(): lax.all_to_all(send, 'expert', split_axis=0, concat_axis=0, tiled=True)  41.8 us
    psum x1, blocking collectives, per_device(): grad_gates = lax.psum(partial_dots, ('pipe', 'tensor'))  38.6 us
    all_to_all x1, waiting for transfers between devices, per_device(): lax.all_to_all(back_send, 'expert', split_axis=0, concat_axis=0, tiled=True)  26.5 us
    all_to_all x1, starting transfers between devices, per_device(): lax.all_to_all(back_send, 'expert', split_axis=0, concat_axis=0, tiled=True)  12.8 us
    unnamed x23, local copies, waits for them, and re-layouts  9.97 us
  transfers between devices with their start and end apart: 5, of which 5 were waited for; matrix products, arithmetic and copies ran while one was open for 2% of the time, Pallas kernels for 0%

commit v1 on v0

--- a/solution.py
+++ b/solution.py
@@ -2,6 +2,11 @@
 import jax.numpy as jnp
 from jax import lax
 from jax.sharding import PartitionSpec as P
+
+
+def axis_by_axis(x, first, second):
+    half = lax.psum(x, first)
+    return lax.psum(half, second)
 
 
 def per_device(tokens, expert_ids, gates, w_gate, w_up, w_down, d_out):
@@ -78,7 +83,7 @@
     moe_out = jnp.sum(gates[:, :, None] * a_out, axis=1).astype(jnp.bfloat16)
     grad_tokens = jnp.sum(a_dx, axis=1).astype(jnp.bfloat16)
     partial_dots = jnp.sum(d_out.astype(jnp.float32)[:, None, :] * a_out, axis=2)
-    grad_gates = lax.psum(partial_dots, ("pipe", "tensor"))
+    grad_gates = axis_by_axis(partial_dots, "tensor", "pipe")
     return (moe_out, grad_tokens, grad_gates)
 
 

time: 458 us -> 440 us (0.961)
  the two profiles are of different devices: /device:TPU:32 before, /device:TPU:2 now
where the time goes in v1:
time: 440 us; the launch traced here: 439 us
  waiting for transfers between devices  321 us (73%)
  blocking collectives  62.4 us (14%)
  between operations  14 us (3%)
  matrix products  13.2 us (3%)
  starting transfers between devices  12.7 us (3%)
  local copies, waits for them, and re-layouts  12.2 us (3%)
    unnamed x6, waiting for transfers between devices  180 us
    all_gather x1, waiting for transfers between devices, per_device(): rows_dy = lax.all_gather(part_dy, ('pipe', 'tensor'), axis=1, tiled=True)  60.3 us
    all_gather x1, waiting for transfers between devices, per_device(): rows_x = lax.all_gather(part_x, ('pipe', 'tensor'), axis=1, tiled=True)  52.8 us
    all_to_all x1, blocking collectives, per_device(): lax.all_to_all(send, 'expert', split_axis=0, concat_axis=0, tiled=True)  43.5 us
    all_to_all x1, waiting for transfers between devices, per_device(): lax.all_to_all(back_send, 'expert', split_axis=0, concat_axis=0, tiled=True)  28.1 us
    all_to_all x1, starting transfers between devices, per_device(): lax.all_to_all(back_send, 'expert', split_axis=0, concat_axis=0, tiled=True)  12.5 us
    psum x1, blocking collectives, axis_by_axis(): return lax.psum(half, second)  10.1 us
    unnamed x23, local copies, waits for them, and re-layouts  9.97 us
  transfers between devices with their start and end apart: 5, of which 5 were waited for; matrix products, arithmetic and copies ran while one was open for 2% of the time, Pallas kernels for 0%

profile of v1, /device:TPU:2, one launch (start us, length us, event | category | flops | bytes accessed | tf_op | source)
XLA Modules:
  0.0 438.9 jit_solution(15398137807818277859)
XLA Ops:
  7.2 0.9 copy.35
  8.7 0.7 multiply_add_fusion
  9.4 0.8 convert_reduce_fusion
  10.1 0.9 convolution_convert_fusion.1
  11.1 0.9 convolution_convert_fusion.2
  12.1 43.5 %all_to_all.10 = bf16[32,5,768]{2,1,0:T(8,128)(2,1)S(1)} all-to-all(bf16[32,5,768]{2,1,0:T(8,128)(2,1)S(1)} %bitcast.32), channel_id=1, replica_groups=mesh['pipe'=4,'expert'=32,'tensor'=4] {'expert'}, dimensions={0} | all-to-all | bytes 491520 | tf_op jit(solution)/shard_map/all_to_all | solution.py:38
  55.7 0.7 fusion.21
  56.5 0.7 all-gather.5.cloned.1.call-update
  57.2 52.8 %all-gather.3.cloned.1.call-done = bf16[160,6144]{1,0:T(8,128)(2,1)} async-done(((bf16[160,384]{1,0:T(8,128)(2,1)}), bf16[160,6144]{1,0:T(8,128)(2,1)}) %all-gather.3.cloned.1.call-update) | async-done | bytes 1966096 | tf_op jit(solution)/shard_map/all_gather | solution.py:42
  110.1 2.3 fusion.9
  112.5 2.2 fusion.5
  114.7 60.3 %all-gather.5.cloned.1.call-done = bf16[160,6144]{1,0:T(8,128)(2,1)} async-done(((bf16[160,384]{1,0:T(8,128)(2,1)}), bf16[160,6144]{1,0:T(8,128)(2,1)}) %all-gather.5.cloned.1.call-update) | async-done | bytes 1966096 | tf_op jit(solution)/shard_map/all_gather | solution.py:43
  174.9 2.2 fusion.1
  177.2 0.7 fusion.7
  177.9 0.7 copy-done.3
  178.6 1.6 fusion
  180.2 2.8 copy.40
  183.0 2.2 convolution_convert_fusion
  185.2 2.8 copy.38
  188.0 85.6 %reduce-scatter.9.cloned.1.call-done = bf16[384,160]{1,0:T(8,128)(2,1)} async-done(((bf16[6144,160]{1,0:T(8,128)(2,1)}), bf16[384,160]{1,0:T(8,128)(2,1)}) %reduce-scatter.9.cloned.1.call-update) | async-done | bytes 122896
  273.6 1.1 copy.41
  274.7 93.5 %reduce-scatter.7.cloned.1.call-done = bf16[384,160]{1,0:T(8,128)(2,1)} async-done(((bf16[6144,160]{1,0:T(8,128)(2,1)}), bf16[384,160]{1,0:T(8,128)(2,1)}) %reduce-scatter.7.cloned.1.call-update) | async-done | bytes 122896
  368.1 1.1 copy.39
  369.2 0.8 reshape.67
  370.1 12.5 %all-to-all-start.1 = ((bf16[32,5,768]{2,1,0:T(8,128)(2,1)}), bf16[32,5,768]{2,1,0:T(8,128)(2,1)S(1)}, u32[]{:S(2)}, u32[]{:S(2)}) async-start(bf16[32,5,768]{2,1,0:T(8,128)(2,1)} %reshape.67), calls=%async_computation.1 | async-start | bytes 786432 | tf_op jit(solution)/shard_map/all_to_all | solution.py:73
  382.8 28.1 %all-to-all-done.1 = bf16[32,5,768]{2,1,0:T(8,128)(2,1)S(1)} async-done(((bf16[32,5,768]{2,1,0:T(8,128)(2,1)}), bf16[32,5,768]{2,1,0:T(8,128)(2,1)S(1)}, u32[]{:S(2)}, u32[]{:S(2)}) %all-to-all-start.1) | async-done | bytes 245792 | tf_op jit(solution)/shard_map/all_to_all | solution.py:73
  411.0 0.2 fusion.15
  411.5 8.8 %psum.14 = f32[16,2]{1,0:T(8,128)S(1)} all-reduce(f32[16,2]{1,0:T(8,128)S(1)} %reduce_sum.72), channel_id=1, replica_groups=mesh['pipe'=4,'expert'=32,'tensor'=4] {'tensor'}, use_global_device_ids=true, to_apply=%region_10.11 | all-reduce | flops 32 | bytes 256 | tf_op jit(solution)/shard_map/psum | solution.py:8
  420.2 10.1 %psum.15 = f32[16,2]{1,0:T(8,128)S(1)} all-reduce(f32[16,2]{1,0:T(8,128)S(1)} %psum.14), channel_id=1, replica_groups=mesh['pipe'=4,'expert'=32,'tensor'=4] {'pipe'}, use_global_device_ids=true, to_apply=%region_11.12 | all-reduce | flops 32 | bytes 256 | tf_op jit(solution)/shard_map/psum | solution.py:9
  430.4 0.6 copy.37
  431.0 0.7 multiply_reduce_fusion.1
  431.7 0.7 reduce_sum.70
  (43 shorter events, 1.5 us)
Async XLA Ops:
  7.2 102.9 %copy-start = (bf16[1,6144,128]{2,1,0:T(8,128)(2,1)S(1)}, bf16[1,6144,128]{2,1,0:T(8,128)(2,1)}, u32[]{:S(2)}) copy-start(bf16[1,6144,128]{2,1,0:T(8,128)(2,1)} %param.10) | copy-start | bytes 4718596
  7.2 102.9 %all-gather.3.cloned.1.call-start = ((), (), s32[]{:S(2)}) async-start(), calls=%async_computation.4 | async-start | bytes 2088960 | tf_op jit(solution)/shard_map/all_gather | solution.py:42
  56.4 118.5 %all-gather.5.cloned.1.call-start = ((), (), s32[]{:S(2)}) async-start(), calls=%async_computation.5 | async-start | bytes 2088960 | tf_op jit(solution)/shard_map/all_gather | solution.py:43
  57.2 216.4 %reduce-scatter.9.cloned.1.call-start = ((), (), s32[]{:S(2)}) async-start(), calls=%async_computation.7 | async-start | bytes 3342336
  110.1 2.4 copy-start.1
  112.4 64.7 %copy-start.4 = (f32[160,128]{1,0:T(8,128)}, f32[160,128]{1,0:T(8,128)S(1)}, u32[]{:S(2)}) copy-start(f32[160,128]{1,0:T(8,128)S(1)} %fusion.9) | copy-start | bytes 245764
  112.5 62.5 %copy-start.2 = (bf16[1,128,6144]{2,1,0:T(8,128)(2,1)S(1)}, bf16[1,128,6144]{2,1,0:T(8,128)(2,1)}, u32[]{:S(2)}) copy-start(bf16[1,128,6144]{2,1,0:T(8,128)(2,1)} %param.12) | copy-start | bytes 4718596
  114.7 62.5 %copy-start.5 = (f32[160,128]{1,0:T(8,128)}, f32[160,128]{1,0:T(8,128)S(1)}, u32[]{:S(2)}) copy-start(f32[160,128]{1,0:T(8,128)S(1)} %fusion.5) | copy-start | bytes 245764
  177.2 1.4 copy-start.3
  182.9 185.2 %reduce-scatter.7.cloned.1.call-start = ((), (), s32[]{:S(2)}) async-start(), calls=%async_computation.6 | async-start | bytes 3342336
  188.0 194.7 %copy-start.7 = (f32[16,2]{0,1:T(2,128)S(1)}, f32[16,2]{0,1:T(2,128)}, u32[]{:S(2)}) copy-start(f32[16,2]{0,1:T(2,128)} %param.9) | copy-start | bytes 388
  188.0 194.7 %copy-start.6 = (bf16[16,384]{1,0:T(8,128)(2,1)S(1)}, bf16[16,384]{1,0:T(8,128)(2,1)}, u32[]{:S(2)}) copy-start(bf16[16,384]{1,0:T(8,128)(2,1)} %param.13) | copy-start | bytes 36868
  370.1 40.8 %all-to-all-start.1 = ((bf16[32,5,768]{2,1,0:T(8,128)(2,1)}), bf16[32,5,768]{2,1,0:T(8,128)(2,1)S(1)}, u32[]{:S(2)}, u32[]{:S(2)}) async-start(bf16[32,5,768]{2,1,0:T(8,128)(2,1)} %reshape.67), calls=%async_computation.1 | async-start | bytes 786432 | tf_op jit(solution)/shard_map/all_to_all | solution.py:73
Sparse Core Ops, SparseCore 0:
  56.6 53.4 all-gather.2
  113.1 61.8 all-gather.4
  183.1 90.4 reduce-scatter.8
  277.7 90.4 reduce-scatter.6
